TPU v7x, 32 devices: a whole 2x2x4 slice. The times are simulated.
32 devices in a mesh: ctx: 4 (over x, core), ep: 8 (over z, y).
Axes of the slice: x: 2, y: 2, z: 4, core: 2. Of those that a mesh axis runs over, the one named last changes fastest.
Arguments:
- query_latent: bfloat16 [1, 512, 128, 512], P(None, 'ctx', 'ep'), may hold values from -6 to 6
- query_rope: bfloat16 [1, 128, 64, 512], P(None, 'ep', None, 'ctx'), may hold values from -12 to 12
- key_latent: bfloat16 [1, 512, 512], P(None, 'ctx'), may hold values from -6 to 6
- key_rope: bfloat16 [1, 64, 512], P(None, None, 'ctx'), may hold values from -14 to 14
- output_grad: bfloat16 [1, 512, 128, 512], P(None, 'ctx', 'ep'), may hold values from -6 to 6
Outputs:
- attended: bfloat16 [1, 512, 128, 512], P(None, 'ctx', 'ep')
- query_latent_grad: bfloat16 [1, 512, 128, 512], P(None, 'ctx', 'ep')
- query_rope_grad: bfloat16 [1, 128, 64, 512], P(None, 'ep', None, 'ctx')
- key_latent_grad: bfloat16 [1, 512, 512], P(None, 'ctx')
- key_rope_grad: bfloat16 [1, 64, 512], P(None, None, 'ctx')
All inputs are finite; a program needn't handle non-finite values.
Results may differ from a plain program's by a relative error of at most 0.018.
Values may be sent and summed in bfloat16 or wider, within the bound.
No kernel may reach another device: no remote copies, remote signals or barrier semaphores. Data moves between devices by JAX's collectives and lax.ppermute only.
A program may use at most 64 MiB of HBM per device.

v0:
```python
import jax
import jax.numpy as jnp
from jax import lax
from jax.sharding import PartitionSpec as P

scale_factor = 192.0 ** (-0.5)


def body(query_latent, query_rope, key_latent, key_rope, output_grad):
    block_len = query_latent.shape[1]
    whole_latent, whole_rope = (
        lax.all_gather(key_latent, "ctx", axis=1, tiled=True),
        lax.all_gather(key_rope, "ctx", axis=2, tiled=True),
    )
    length = whole_latent.shape[1]
    offset = lax.axis_index("ctx") * block_len
    query_place = offset + jnp.arange(block_len, dtype=jnp.int32)
    allowed = jnp.arange(length, dtype=jnp.int32)[None, :] <= query_place[:, None]
    scores = jnp.einsum(
        "sthd,sjd->shtj", query_latent, whole_latent, preferred_element_type=jnp.float32
    )
    scores = scores + jnp.einsum(
        "shdt,sdj->shtj", query_rope, whole_rope, preferred_element_type=jnp.float32
    )
    scores = jnp.where(allowed, scores * scale_factor, jnp.float32(-1e30))
    row_max = jnp.max(scores, axis=-1, keepdims=True)
    powers = jnp.exp(scores - row_max)
    weights = powers / jnp.sum(powers, axis=-1, keepdims=True)
    rounded_weights = weights.astype(jnp.bfloat16)
    attended = jnp.einsum(
        "shtj,sjd->sthd", rounded_weights, whole_latent, preferred_element_type=jnp.float32
    ).astype(jnp.bfloat16)
    row_dots = jnp.einsum(
        "sthd,sthd->sht", output_grad, attended, preferred_element_type=jnp.float32
    )
    weight_grad = jnp.einsum(
        "sthd,sjd->shtj", output_grad, whole_latent, preferred_element_type=jnp.float32
    )
    score_grad = (weights * (weight_grad - row_dots[..., None])).astype(jnp.bfloat16)
    latent_qgrad = (
        scale_factor
        * jnp.einsum("shtj,sjd->sthd", score_grad, whole_latent, preferred_element_type=jnp.float32)
    ).astype(jnp.bfloat16)
    rope_qgrad = (
        scale_factor
        * jnp.einsum("shtj,sdj->shdt", score_grad, whole_rope, preferred_element_type=jnp.float32)
    ).astype(jnp.bfloat16)
    latent_term = scale_factor * jnp.einsum(
        "shtj,sthd->sjd", score_grad, query_latent, preferred_element_type=jnp.float32
    )
    latent_term = latent_term + jnp.einsum(
        "shtj,sthd->sjd", rounded_weights, output_grad, preferred_element_type=jnp.float32
    )
    rope_term = scale_factor * jnp.einsum(
        "shtj,shdt->sdj", score_grad, query_rope, preferred_element_type=jnp.float32
    )
    latent_part, rope_part = (
        lax.psum_scatter(
            latent_term.astype(jnp.bfloat16), "ctx", scatter_dimension=1, tiled=True
        ).astype(jnp.float32),
        lax.psum_scatter(
            rope_term.astype(jnp.bfloat16), "ctx", scatter_dimension=2, tiled=True
        ).astype(jnp.float32),
    )
    latent_total, rope_total = (
        lax.psum(latent_part.astype(jnp.bfloat16), "ep").astype(jnp.float32),
        lax.psum(rope_part.astype(jnp.bfloat16), "ep").astype(jnp.float32),
    )
    latent_kgrad = latent_total.astype(jnp.bfloat16)
    rope_kgrad = rope_total.astype(jnp.bfloat16)
    return (attended, latent_qgrad, rope_qgrad, latent_kgrad, rope_kgrad)


def solution(mesh):
    placed = (
        P(None, "ctx", "ep", None),
        P(None, "ep", None, "ctx"),
        P(None, "ctx", None),
        P(None, None, "ctx"),
        P(None, "ctx", "ep", None),
    )
    return jax.shard_map(
        body,
        mesh=mesh,
        in_specs=placed,
        out_specs=(
            P(None, "ctx", "ep", None),
            P(None, "ctx", "ep", None),
            P(None, "ep", None, "ctx"),
            P(None, "ctx", None),
            P(None, None, "ctx"),
        ),
        check_vma=False,
    )
```

profile of v0, /device:TPU:0, one launch (start us, length us, event | category | flops | bytes accessed | tf_op | source)
XLA Modules:
  0.0 172.1 jit_solution(7928292447915737085)
XLA Ops:
  7.2 0.0 copy-start
  7.2 0.0 reduce-scatter.5.cloned.1.call-start
  7.2 9.0 %all_gather.6 = bf16[1,512,512]{2,1,0:T(8,128)(2,1)S(1)} all-gather(bf16[1,128,512]{2,1,0:T(8,128)(2,1)} %param.7), channel_id=1, replica_groups=mesh['ctx'=4,'ep'=8] {'ctx'}, dimensions={1}, use_global_device_ids=true | all-gather | bytes 655360 | tf_op jit(solution)/shard_map/all_gather | solution.py:12
  16.2 5.5 %all_gather.7 = bf16[1,64,512]{2,1,0:T(8,128)(2,1)S(1)} all-gather(bf16[1,64,128]{2,1,0:T(8,128)(2,1)} %param.8), channel_id=1, replica_groups=mesh['ctx'=4,'ep'=8] {'ctx'}, dimensions={2}, use_global_device_ids=true | all-gather | bytes 81920 | tf_op jit(solution)/shard_map/all_gather | solution.py:13
  21.7 0.1 iota_compare_fusion
  21.7 0.0 copy-done
  21.7 0.0 copy-start.7
  21.7 2.8 %fusion.23 = f32[512,128,16]{1,0,2:T(8,128)S(1)} fusion(bf16[128,16,512]{2,1,0:T(8,128)(2,1)S(1)} %bitcast.149, bf16[1,512,512]{2,1,0:T(8,128)(2,1)S(1)} %all_gather.6), kind=kOutput, calls=%fused_computation.26 | convolution fusion | flops 1073741824 | bytes 6815744 | tf_op jit(solution)/shard_map/sthd,sjd->shtj/dot_general | solution.py:19
  24.5 0.0 copy-done.7
  24.6 0.9 fusion.90
  25.5 0.0 copy-start.2
  25.5 0.6 fusion.5
  26.1 0.0 copy-start.4
  26.1 2.6 %fusion.91 = (f32[16,128,512]{2,1,0:T(8,128)S(1)}, bf16[16,128,512]{2,1,0:T(8,128)(2,1)}) fusion(bf16[1,512,512]{2,1,0:T(8,128)(2,1)S(1)} %all_gather.6, f32[16,128]{1,0:T(8,128)S(1)} %fusion.5, f32[1,16,128,512]{2,3,1,0:T(8,128)S(1)} %get-tuple-element.16, f32[16,128]{1,0:T(8,128)S(1)} %get-tuple-element.15), kind=kOutput, calls=%fused_computation.56 | convolution fusion | flops 1078984704 | bytes 11026432 | tf_op jit(solution)/shard_map/shtj,sjd->sthd/dot_general | solution.py:30
  28.7 0.0 copy-done.2
  28.7 0.2 copy-done.4
  28.9 2.4 %multiply_reduce_fusion = f32[16,128]{0,1:T(8,128)S(1)} fusion(f32[16,128,512]{2,1,0:T(8,128)S(1)} %get-tuple-element.17, bf16[1,128,16,512]{3,2,1,0:T(8,128)(2,1)S(1)} %copy-done.4), kind=kLoop, calls=%fused_computation.6 | loop fusion | flops 3143680 | bytes 6299648
  31.3 0.1 copy.40
  31.4 0.0 copy-start.3
  31.4 0.0 copy-start.5
  31.4 5.8 %fusion.28 = f32[512,512]{1,0:T(8,128)S(1)} fusion(bf16[128,16,512]{2,1,0:T(8,128)(2,1)} %bitcast.151, f32[16,128]{1,0:T(8,128)S(1)} %fusion.5, f32[1,16,128,512]{2,3,1,0:T(8,128)} %copy-done.2, f32[16,128]{1,0:T(8,128)S(1)} %get-tuple-element.15), kind=kOutput, calls=%fused_computation.29 | convolution fusion | flops 1076887552 | bytes 7356416 | tf_op jit(solution)/shard_map/shtj,sthd->sjd/dot_general | solution.py:51
  37.2 0.0 copy-done.3
  37.2 0.0 copy-done.5
  37.2 3.6 %fusion.1 = bf16[1,16,128,512]{2,3,1,0:T(8,128)(2,1)S(1)} fusion(f32[16,128]{1,0:T(8,128)S(1)} %copy.40, bf16[128,16,512]{2,1,0:T(8,128)(2,1)S(1)} %bitcast.152, f32[16,128]{1,0:T(8,128)S(1)} %fusion.5, f32[1,16,128,512]{2,3,1,0:T(8,128)S(1)} %copy-done.3, f32[16,128]{1,0:T(8,128)S(1)} %get-tuple-element.15, bf16[1,512,512]{2,1,0:T(8,128)(2,1)S(1)} %all_gather.6), kind=kOutput, calls=%fused_computation.2 | convolution fusion | flops 1078984704 | bytes 8937472 | tf_op jit(solution)/shard_map/sthd,sjd->shtj/dot_general | solution.py:36
  40.8 0.0 copy-start.1
  40.8 1.3 copy-done.1
  42.1 3.4 %fusion.53 = bf16[1,512,512]{2,1,0:T(8,128)(2,1)} fusion(f32[512,512]{1,0:T(8,128)S(1)} %fusion.28, bf16[128,16,512]{2,1,0:T(8,128)(2,1)S(1)} %bitcast.150, bf16[1,16,128,512]{2,3,1,0:T(8,128)(2,1)S(1)} %fusion.1), kind=kOutput, calls=%fused_computation.34 | convolution fusion | flops 1074528256 | bytes 5767168 | tf_op jit(solution)/shard_map/shtj,sthd->sjd/dot_general | solution.py:48
  45.5 0.0 reduce-scatter.5.cloned.1.call-update
  45.5 0.0 reduce-scatter.7.cloned.1.call-start
  45.6 2.3 %fusion.77 = bf16[1,64,512]{2,1,0:T(8,128)(2,1)S(1)} fusion(bf16[1,16,128,512]{2,3,1,0:T(8,128)(2,1)} %copy-done.1, bf16[1,16,64,128]{3,2,1,0:T(8,128)(2,1)S(1)} %copy-done.7), kind=kOutput, calls=%fused_computation.42 | convolution fusion | flops 134283264 | bytes 2424832 | tf_op jit(solution)/shard_map/shtj,shdt->sdj/dot_general | solution.py:54
  47.9 0.2 copy.44
  48.1 0.7 copy.69
  48.8 0.0 reduce-scatter.7.cloned.1.call-update
  48.8 0.0 all-reduce.2.cloned.1.call-start
  48.9 4.2 %fusion.25 = bf16[1,128,16,512]{3,1,2,0:T(8,128)(2,1)} fusion(bf16[1,16,128,512]{2,3,1,0:T(8,128)(2,1)} %copy-done.1, bf16[1,512,512]{2,1,0:T(8,128)(2,1)S(1)} %all_gather.6), kind=kOutput, calls=%fused_computation.28 | convolution fusion | flops 1075838976 | bytes 4718592 | tf_op jit(solution)/shard_map/shtj,sjd->sthd/dot_general | solution.py:42
  53.1 15.1 %reduce-scatter.5.cloned.1.call-done = bf16[1,128,512]{2,1,0:T(8,128)(2,1)} async-done(((bf16[1,512,512]{2,1,0:T(8,128)(2,1)}), bf16[1,128,512]{2,1,0:T(8,128)(2,1)}) %reduce-scatter.5.cloned.1.call-update) | async-done | bytes 131088 | tf_op jit(solution)/shard_map/reduce_scatter | solution.py:58
  68.2 0.0 all-reduce.2.cloned.1.call-update
  68.3 0.0 copy-start.6
  68.3 2.9 %fusion.65 = bf16[1,16,64,128]{3,2,1,0:T(8,128)(2,1)} fusion(bf16[1,16,128,512]{2,3,1,0:T(8,128)(2,1)} %copy-done.1, bf16[1,64,512]{2,1,0:T(8,128)(2,1)S(1)} %all_gather.7), kind=kOutput, calls=%fused_computation.38 | convolution fusion | flops 134479872 | bytes 2424832 | tf_op jit(solution)/shard_map/shtj,sdj->shdt/dot_general | solution.py:46
  71.2 4.1 %copy.31 = bf16[1,128,16,512]{3,2,1,0:T(8,128)(2,1)} copy(bf16[1,128,16,512]{3,1,2,0:T(8,128)(2,1)} %fusion.25) | data formatting | bytes 4194304
  75.3 0.0 copy-done.6
  75.3 2.5 %copy.30 = bf16[1,128,16,512]{3,2,1,0:T(8,128)(2,1)} copy(bf16[1,128,16,512]{3,1,2,0:T(8,128)(2,1)S(1)} %bitcast.153) | data formatting | bytes 4194304
  77.8 13.2 %reduce-scatter.7.cloned.1.call-done = bf16[128,64]{1,0:T(8,128)(2,1)} async-done(((bf16[512,64]{1,0:T(8,128)(2,1)}), bf16[128,64]{1,0:T(8,128)(2,1)}) %reduce-scatter.7.cloned.1.call-update) | async-done | bytes 16400
  91.0 0.8 reshape_bitcast_fusion
  91.8 0.1 copy.45
  91.9 37.7 %psum.15 = bf16[1,64,128]{2,1,0:T(8,128)(2,1)} all-reduce(bf16[1,64,128]{2,1,0:T(8,128)(2,1)S(1)} %copy.45), channel_id=1, replica_groups=mesh['ctx'=4,'ep'=8] {'ep'}, use_global_device_ids=true, to_apply=%region_5.6 | all-reduce | flops 8192 | bytes 32768 | tf_op jit(solution)/shard_map/psum | solution.py:67
  129.6 34.5 %all-reduce.2.cloned.1.call-done = bf16[1,128,512]{2,1,0:T(8,128)(2,1)} async-done(((bf16[1,128,512]{2,1,0:T(8,128)(2,1)}), bf16[1,128,512]{2,1,0:T(8,128)(2,1)}) %all-reduce.2.cloned.1.call-update) | async-done | bytes 131088 | tf_op jit(solution)/shard_map/psum | solution.py:66
  164.0 1.6 copy.71
  (1 shorter events, 0.0 us)
Async XLA Ops:
  7.2 14.6 %copy-start = (bf16[1,128,16,512]{3,2,1,0:T(8,128)(2,1)S(1)}, bf16[1,128,16,512]{3,2,1,0:T(8,128)(2,1)}, u32[]{:S(2)}) copy-start(bf16[1,128,16,512]{3,2,1,0:T(8,128)(2,1)} %param.5) | copy-start | bytes 6291460
  7.2 61.1 %reduce-scatter.5.cloned.1.call-start = ((), (), s32[]{:S(2)}) async-start(), calls=%async_computation.2 | async-start | bytes 655360 | tf_op jit(solution)/shard_map/reduce_scatter | solution.py:58
  21.7 2.8 %copy-start.7 = (bf16[1,16,64,128]{3,2,1,0:T(8,128)(2,1)S(1)}, bf16[1,16,64,128]{3,2,1,0:T(8,128)(2,1)}, u32[]{:S(2)}) copy-start(bf16[1,16,64,128]{3,2,1,0:T(8,128)(2,1)} %param.6) | copy-start | bytes 786436
  25.5 3.3 %copy-start.2 = (f32[1,16,128,512]{2,3,1,0:T(8,128)}, f32[1,16,128,512]{2,3,1,0:T(8,128)S(1)}, u32[]{:S(2)}) copy-start(f32[1,16,128,512]{2,3,1,0:T(8,128)S(1)} %get-tuple-element.16) | copy-start | bytes 12582916
  26.1 2.9 %copy-start.4 = (bf16[1,128,16,512]{3,2,1,0:T(8,128)(2,1)S(1)}, bf16[1,128,16,512]{3,2,1,0:T(8,128)(2,1)}, u32[]{:S(2)}) copy-start(bf16[1,128,16,512]{3,2,1,0:T(8,128)(2,1)} %param.9) | copy-start | bytes 6291460
  31.4 5.8 %copy-start.3 = (f32[1,16,128,512]{2,3,1,0:T(8,128)S(1)}, f32[1,16,128,512]{2,3,1,0:T(8,128)}, u32[]{:S(2)}) copy-start(f32[1,16,128,512]{2,3,1,0:T(8,128)} %copy-done.2) | copy-start | bytes 12582916
  31.4 5.8 %copy-start.5 = (bf16[1,128,16,512]{3,2,1,0:T(8,128)(2,1)S(1)}, bf16[1,128,16,512]{3,2,1,0:T(8,128)(2,1)}, u32[]{:S(2)}) copy-start(bf16[1,128,16,512]{3,2,1,0:T(8,128)(2,1)} %param.9) | copy-start | bytes 6291460
  40.8 1.3 copy-start.1
  45.5 45.5 %reduce-scatter.7.cloned.1.call-start = ((), (), s32[]{:S(2)}) async-start(), calls=%async_computation.4 | async-start | bytes 163840
  48.8 115.2 %all-reduce.2.cloned.1.call-start = ((), (), s32[]{:S(2)}) async-start(), calls=%async_computation.3 | async-start | bytes 262144 | tf_op jit(solution)/shard_map/psum | solution.py:66
  68.3 7.0 %copy-start.6 = (bf16[16,128,512]{2,1,0:T(8,128)(2,1)S(1)}, bf16[16,128,512]{2,1,0:T(8,128)(2,1)}, u32[]{:S(2)}) copy-start(bf16[16,128,512]{2,1,0:T(8,128)(2,1)} %get-tuple-element.18) | copy-start | bytes 6291460
Sparse Core Ops, SparseCore 0:
  45.7 22.5 reduce-scatter.4
  71.4 19.5 reduce-scatter.6
  94.3 69.6 all-reduce.1
where the time goes:
time: 173 us; the launch traced here: 172 us
  waiting for transfers between devices  62.9 us (36%)
  blocking collectives  52.1 us (30%)
  matrix products  28.6 us (17%)
  between operations  13.9 us (8%)
  local copies, waits for them, and re-layouts  11.5 us (7%)
  other arithmetic  3.03 us (2%)
    psum x1, blocking collectives, body(): lax.psum(rope_part.astype(jnp.bfloat16), 'ep').astype(jnp.float32)  37.7 us
    psum x1, waiting for transfers between devices, body(): lax.psum(latent_part.astype(jnp.bfloat16), 'ep').astype(jnp.float32)  34.5 us
    reduce_scatter x1, waiting for transfers between devices, body(): lax.psum_scatter(latent_term.astype(jnp.bfloat16), 'ctx', scatter_dimensi...  15.1 us
    unnamed x4, waiting for transfers between devices  13.3 us
    unnamed x23, local copies, waits for them, and re-layouts  11.4 us
    all_gather x1, blocking collectives, body(): lax.all_gather(key_latent, 'ctx', axis=1, tiled=True)  8.96 us
    dot_general x1, matrix products, body(): jnp.einsum('shtj,sthd->sjd', rounded_weights, output_grad, preferred_elem...  5.81 us
    all_gather x1, blocking collectives, body(): lax.all_gather(key_rope, 'ctx', axis=2, tiled=True)  5.46 us
  transfers between devices with their start and end apart: 3, of which 3 were waited for; matrix products, arithmetic and copies ran while one was open for 10% of the time, Pallas kernels for 0%

commit v1 on v0

--- a/solution.py
+++ b/solution.py
@@ -63,7 +63,7 @@
         ).astype(jnp.float32),
     )
     latent_total, rope_total = (
-        lax.psum(latent_part.astype(jnp.bfloat16), "ep").astype(jnp.float32),
+        jnp.sum(lax.all_gather(latent_part.astype(jnp.bfloat16), "ep"), axis=0).astype(jnp.float32),
         lax.psum(rope_part.astype(jnp.bfloat16), "ep").astype(jnp.float32),
     )
     latent_kgrad = latent_total.astype(jnp.bfloat16)

time: 173 us -> 142 us (0.82)
  waiting for transfers between devices: 62.9 us -> 36.4 us
  local copies, waits for them, and re-layouts: 11.5 us -> 8.34 us
  matrix products: 28.6 us -> 25.7 us
  other arithmetic: 3.03 us -> 5.09 us
    psum x1 -> x0, waiting for transfers between devices: 34.5 us -> none  [body(): lax.psum(latent_part.astype(jnp.bfloat16), 'ep').astype(jnp.float32)]
    reduce_scatter x1, waiting for transfers between devices: 15.1 us -> 19.4 us  [body(): lax.psum_scatter(latent_term.astype(jnp.bfloat16), 'ctx', scatter_dimensi...]
    all_gather x0 -> x1, waiting for transfers between devices: none -> 3.44 us  [body(): lax.all_gather(latent_part.astype(jnp.bfloat16), 'ep')]
    unnamed x23 -> x24, local copies, waits for them, and re-layouts: 11.4 us -> 8.27 us
    reduce_sum x0 -> x1, other arithmetic: none -> 2.06 us  [body(): jnp.sum(lax.all_gather(latent_part.astype(jnp.bfloat16), 'ep'), axis=0)]
    dot_general x1, matrix products: 2.93 us -> 1.19 us  [body(): jnp.einsum('shtj,sdj->shdt', score_grad, whole_rope, preferred_element_ty...]
  transfers between devices with their start and end apart: 3 -> 3, of which waited for: 3 -> 3; matrix products, arithmetic and copies ran while one was open for 10% -> 9% of each run, Pallas kernels for 0% -> 0%
where the time goes in v1:
time: 142 us
  blocking collectives  52.5 us (37%)
  waiting for transfers between devices  36.4 us (26%)
  matrix products  25.7 us (18%)
  between operations  13.9 us (10%)
  local copies, waits for them, and re-layouts  8.34 us (6%)
  other arithmetic  5.09 us (4%)
    psum x1, blocking collectives, body(): lax.psum(rope_part.astype(jnp.bfloat16), 'ep').astype(jnp.float32)  38.1 us
    reduce_scatter x1, waiting for transfers between devices, body(): lax.psum_scatter(latent_term.astype(jnp.bfloat16), 'ctx', scatter_dimensi...  19.4 us
    unnamed x4, waiting for transfers between devices  13.6 us
    all_gather x1, blocking collectives, body(): lax.all_gather(key_latent, 'ctx', axis=1, tiled=True)  8.96 us
    unnamed x24, local copies, waits for them, and re-layouts  8.27 us
    dot_general x1, matrix products, body(): jnp.einsum('shtj,sthd->sjd', rounded_weights, output_grad, preferred_elem...  5.81 us
    all_gather x1, blocking collectives, body(): lax.all_gather(key_rope, 'ctx', axis=2, tiled=True)  5.46 us
    dot_general x1, matrix products, body(): jnp.einsum('sthd,sjd->shtj', output_grad, whole_latent, preferred_element...  3.58 us
  transfers between devices with their start and end apart: 3, of which 3 were waited for; matrix products, arithmetic and copies ran while one was open for 9% of the time, Pallas kernels for 0%

profile of v1, /device:TPU:0, one launch (start us, length us, event | category | flops | bytes accessed | tf_op | source)
XLA Modules:
  0.0 142.0 jit_solution(3787447948937611190)
XLA Ops:
  7.2 0.0 copy-start
  7.2 0.0 reduce-scatter.5.cloned.1.call-start
  7.2 9.0 %all_gather.12 = bf16[1,512,512]{2,1,0:T(8,128)(2,1)S(1)} all-gather(bf16[1,128,512]{2,1,0:T(8,128)(2,1)} %param.7), channel_id=1, replica_groups=mesh['ctx'=4,'ep'=8] {'ctx'}, dimensions={1}, use_global_device_ids=true | all-gather | bytes 655360 | tf_op jit(solution)/shard_map/all_gather | solution.py:12
  16.2 5.5 %all_gather.13 = bf16[1,64,512]{2,1,0:T(8,128)(2,1)S(1)} all-gather(bf16[1,64,128]{2,1,0:T(8,128)(2,1)} %param.8), channel_id=1, replica_groups=mesh['ctx'=4,'ep'=8] {'ctx'}, dimensions={2}, use_global_device_ids=true | all-gather | bytes 81920 | tf_op jit(solution)/shard_map/all_gather | solution.py:13
  21.7 0.1 iota_compare_fusion
  21.7 0.0 copy-done
  21.7 0.0 copy-start.8
  21.7 2.8 %fusion.23 = f32[512,128,16]{1,0,2:T(8,128)S(1)} fusion(bf16[128,16,512]{2,1,0:T(8,128)(2,1)S(1)} %bitcast.150, bf16[1,512,512]{2,1,0:T(8,128)(2,1)S(1)} %all_gather.12), kind=kOutput, calls=%fused_computation.26 | convolution fusion | flops 1073741824 | bytes 6815744 | tf_op jit(solution)/shard_map/sthd,sjd->shtj/dot_general | solution.py:19
  24.5 0.0 copy-done.8
  24.6 0.9 fusion.90
  25.5 0.0 copy-start.3
  25.5 0.6 fusion.5
  26.1 0.0 copy-start.5
  26.1 2.6 %fusion.91 = (f32[16,128,512]{2,1,0:T(8,128)S(1)}, bf16[16,128,512]{2,1,0:T(8,128)(2,1)}) fusion(bf16[1,512,512]{2,1,0:T(8,128)(2,1)S(1)} %all_gather.12, f32[16,128]{1,0:T(8,128)S(1)} %fusion.5, f32[1,16,128,512]{2,3,1,0:T(8,128)S(1)} %get-tuple-element.16, f32[16,128]{1,0:T(8,128)S(1)} %get-tuple-element.15), kind=kOutput, calls=%fused_computation.56 | convolution fusion | flops 1078984704 | bytes 11026432 | tf_op jit(solution)/shard_map/shtj,sjd->sthd/dot_general | solution.py:30
  28.7 0.0 copy-done.3
  28.7 0.2 copy-done.5
  28.9 2.4 %multiply_reduce_fusion = f32[16,128]{0,1:T(8,128)S(1)} fusion(f32[16,128,512]{2,1,0:T(8,128)S(1)} %get-tuple-element.17, bf16[1,128,16,512]{3,2,1,0:T(8,128)(2,1)S(1)} %copy-done.5), kind=kLoop, calls=%fused_computation.6 | loop fusion | flops 3143680 | bytes 6299648
  31.3 0.1 copy.40
  31.4 0.0 copy-start.4
  31.4 0.0 copy-start.6
  31.4 5.8 %fusion.28 = f32[512,512]{1,0:T(8,128)S(1)} fusion(bf16[128,16,512]{2,1,0:T(8,128)(2,1)} %bitcast.152, f32[16,128]{1,0:T(8,128)S(1)} %fusion.5, f32[1,16,128,512]{2,3,1,0:T(8,128)} %copy-done.3, f32[16,128]{1,0:T(8,128)S(1)} %get-tuple-element.15), kind=kOutput, calls=%fused_computation.29 | convolution fusion | flops 1076887552 | bytes 7356416 | tf_op jit(solution)/shard_map/shtj,sthd->sjd/dot_general | solution.py:51
  37.2 0.0 copy-done.4
  37.2 0.0 copy-done.6
  37.2 3.6 %fusion.1 = bf16[1,16,128,512]{2,3,1,0:T(8,128)(2,1)S(1)} fusion(f32[16,128]{1,0:T(8,128)S(1)} %copy.40, bf16[128,16,512]{2,1,0:T(8,128)(2,1)S(1)} %bitcast.153, f32[16,128]{1,0:T(8,128)S(1)} %fusion.5, f32[1,16,128,512]{2,3,1,0:T(8,128)S(1)} %copy-done.4, f32[16,128]{1,0:T(8,128)S(1)} %get-tuple-element.15, bf16[1,512,512]{2,1,0:T(8,128)(2,1)S(1)} %all_gather.12), kind=kOutput, calls=%fused_computation.2 | convolution fusion | flops 1078984704 | bytes 8937472 | tf_op jit(solution)/shard_map/sthd,sjd->shtj/dot_general | solution.py:36
  40.8 0.0 copy-start.1
  40.8 1.3 copy-done.1
  42.2 3.4 %fusion.53 = bf16[1,512,512]{2,1,0:T(8,128)(2,1)} fusion(f32[512,512]{1,0:T(8,128)S(1)} %fusion.28, bf16[128,16,512]{2,1,0:T(8,128)(2,1)S(1)} %bitcast.151, bf16[1,16,128,512]{2,3,1,0:T(8,128)(2,1)S(1)} %fusion.1), kind=kOutput, calls=%fused_computation.34 | convolution fusion | flops 1074528256 | bytes 5767168 | tf_op jit(solution)/shard_map/shtj,sthd->sjd/dot_general | solution.py:48
  45.5 0.0 reduce-scatter.5.cloned.1.call-update
  45.6 0.0 reduce-scatter.7.cloned.1.call-start
  45.6 2.3 %fusion.77 = bf16[1,64,512]{2,1,0:T(8,128)(2,1)S(1)} fusion(bf16[1,16,128,512]{2,3,1,0:T(8,128)(2,1)} %copy-done.1, bf16[1,16,64,128]{3,2,1,0:T(8,128)(2,1)S(1)} %copy-done.8), kind=kOutput, calls=%fused_computation.42 | convolution fusion | flops 134283264 | bytes 2424832 | tf_op jit(solution)/shard_map/shtj,shdt->sdj/dot_general | solution.py:54
  48.0 0.2 copy.44
  48.1 0.7 copy.69
  48.8 0.0 reduce-scatter.7.cloned.1.call-update
  48.8 0.0 all-gather.3.cloned.1.call-start
  48.9 19.4 %reduce-scatter.5.cloned.1.call-done = bf16[1,128,512]{2,1,0:T(8,128)(2,1)} async-done(((bf16[1,512,512]{2,1,0:T(8,128)(2,1)}), bf16[1,128,512]{2,1,0:T(8,128)(2,1)}) %reduce-scatter.5.cloned.1.call-update) | async-done | bytes 131088 | tf_op jit(solution)/shard_map/reduce_scatter | solution.py:58
  68.2 0.0 all-gather.3.cloned.1.call-update
  68.3 0.0 copy-start.7
  68.3 3.0 %fusion.25 = bf16[1,128,16,512]{3,1,2,0:T(8,128)(2,1)S(1)} fusion(bf16[1,16,128,512]{2,3,1,0:T(8,128)(2,1)} %copy-done.1, bf16[1,512,512]{2,1,0:T(8,128)(2,1)S(1)} %all_gather.12), kind=kOutput, calls=%fused_computation.28 | convolution fusion | flops 1075838976 | bytes 4718592 | tf_op jit(solution)/shard_map/shtj,sjd->sthd/dot_general | solution.py:42
  71.3 0.0 copy-start.2
  71.3 2.5 %copy.31 = bf16[1,128,16,512]{3,2,1,0:T(8,128)(2,1)} copy(bf16[1,128,16,512]{3,1,2,0:T(8,128)(2,1)S(1)} %fusion.25) | data formatting | bytes 4194304
  73.8 0.0 copy-done.7
  73.8 2.5 %copy.30 = bf16[1,128,16,512]{3,2,1,0:T(8,128)(2,1)} copy(bf16[1,128,16,512]{3,1,2,0:T(8,128)(2,1)S(1)} %bitcast.154) | data formatting | bytes 4194304
  76.3 0.0 copy-done.2
  76.3 1.2 fusion.65
  77.5 13.5 %reduce-scatter.7.cloned.1.call-done = bf16[128,64]{1,0:T(8,128)(2,1)} async-done(((bf16[512,64]{1,0:T(8,128)(2,1)}), bf16[128,64]{1,0:T(8,128)(2,1)}) %reduce-scatter.7.cloned.1.call-update) | async-done | bytes 16400
  91.0 0.8 reshape_bitcast_fusion
  91.8 0.1 copy.45
  91.9 38.1 %psum.7 = bf16[1,64,128]{2,1,0:T(8,128)(2,1)} all-reduce(bf16[1,64,128]{2,1,0:T(8,128)(2,1)S(1)} %copy.45), channel_id=1, replica_groups=mesh['ctx'=4,'ep'=8] {'ep'}, use_global_device_ids=true, to_apply=%region_5.6 | all-reduce | flops 8192 | bytes 32768 | tf_op jit(solution)/shard_map/psum | solution.py:67
  129.9 3.4 %all-gather.3.cloned.1.call-done = bf16[8,128,512]{2,1,0:T(8,128)(2,1)} async-done(((bf16[1,128,512]{2,1,0:T(8,128)(2,1)}), bf16[8,128,512]{2,1,0:T(8,128)(2,1)}) %all-gather.3.cloned.1.call-update) | async-done | bytes 1048592 | tf_op jit(solution)/shard_map/all_gather | solution.py:66
  133.4 2.1 %reduce.4 = bf16[128,512]{1,0:T(8,128)(2,1)} reduce(bf16[8,128,512]{2,1,0:T(8,128)(2,1)} %all-gather.3.cloned.1.call-done, bf16[]{:T(256)} %constant.5.clone.1), dimensions={0}, to_apply=%region_3.4 | reduce | flops 458752 | bytes 1179650 | tf_op jit(solution)/shard_map/reduce_sum | solution.py:66
  (1 shorter events, 0.0 us)
Async XLA Ops:
  7.2 14.6 %copy-start = (bf16[1,128,16,512]{3,2,1,0:T(8,128)(2,1)S(1)}, bf16[1,128,16,512]{3,2,1,0:T(8,128)(2,1)}, u32[]{:S(2)}) copy-start(bf16[1,128,16,512]{3,2,1,0:T(8,128)(2,1)} %param.5) | copy-start | bytes 6291460
  7.2 61.1 %reduce-scatter.5.cloned.1.call-start = ((), (), s32[]{:S(2)}) async-start(), calls=%async_computation.2 | async-start | bytes 655360 | tf_op jit(solution)/shard_map/reduce_scatter | solution.py:58
  21.7 2.8 %copy-start.8 = (bf16[1,16,64,128]{3,2,1,0:T(8,128)(2,1)S(1)}, bf16[1,16,64,128]{3,2,1,0:T(8,128)(2,1)}, u32[]{:S(2)}) copy-start(bf16[1,16,64,128]{3,2,1,0:T(8,128)(2,1)} %param.6) | copy-start | bytes 786436
  25.5 3.3 %copy-start.3 = (f32[1,16,128,512]{2,3,1,0:T(8,128)}, f32[1,16,128,512]{2,3,1,0:T(8,128)S(1)}, u32[]{:S(2)}) copy-start(f32[1,16,128,512]{2,3,1,0:T(8,128)S(1)} %get-tuple-element.16) | copy-start | bytes 12582916
  26.1 2.9 %copy-start.5 = (bf16[1,128,16,512]{3,2,1,0:T(8,128)(2,1)S(1)}, bf16[1,128,16,512]{3,2,1,0:T(8,128)(2,1)}, u32[]{:S(2)}) copy-start(bf16[1,128,16,512]{3,2,1,0:T(8,128)(2,1)} %param.9) | copy-start | bytes 6291460
  31.4 5.8 %copy-start.4 = (f32[1,16,128,512]{2,3,1,0:T(8,128)S(1)}, f32[1,16,128,512]{2,3,1,0:T(8,128)}, u32[]{:S(2)}) copy-start(f32[1,16,128,512]{2,3,1,0:T(8,128)} %copy-done.3) | copy-start | bytes 12582916
  31.4 5.8 %copy-start.6 = (bf16[1,128,16,512]{3,2,1,0:T(8,128)(2,1)S(1)}, bf16[1,128,16,512]{3,2,1,0:T(8,128)(2,1)}, u32[]{:S(2)}) copy-start(bf16[1,128,16,512]{3,2,1,0:T(8,128)(2,1)} %param.9) | copy-start | bytes 6291460
  40.8 1.4 copy-start.1
  45.6 45.4 %reduce-scatter.7.cloned.1.call-start = ((), (), s32[]{:S(2)}) async-start(), calls=%async_computation.4 | async-start | bytes 163840
  48.8 84.6 %all-gather.3.cloned.1.call-start = ((), (), s32[]{:S(2)}) async-start(), calls=%async_computation.3 | async-start | bytes 1179648 | tf_op jit(solution)/shard_map/all_gather | solution.py:66
  68.3 5.5 %copy-start.7 = (bf16[16,128,512]{2,1,0:T(8,128)(2,1)S(1)}, bf16[16,128,512]{2,1,0:T(8,128)(2,1)}, u32[]{:S(2)}) copy-start(bf16[16,128,512]{2,1,0:T(8,128)(2,1)} %get-tuple-element.18) | copy-start | bytes 6291460
  71.3 5.0 %copy-start.2 = (bf16[1,16,128,512]{2,3,1,0:T(8,128)(2,1)S(1)}, bf16[1,16,128,512]{2,3,1,0:T(8,128)(2,1)}, u32[]{:S(2)}) copy-start(bf16[1,16,128,512]{2,3,1,0:T(8,128)(2,1)} %copy-done.1) | copy-start | bytes 6291460
Sparse Core Ops, SparseCore 0:
  45.7 22.5 reduce-scatter.4
  71.4 19.5 reduce-scatter.6
  93.1 40.2 all-gather.2
